TPU v7x, 32 devices: a whole 2x2x4 slice. The times are simulated.
32 devices in a mesh: ctx: 4 (over x, core), ep: 8 (over z, y).
Axes of the slice: x: 2, y: 2, z: 4, core: 2. Of those that a mesh axis runs over, the one named last changes fastest.
Arguments:
- query_latent: bfloat16 [1, 512, 128, 512], P(None, 'ctx', 'ep'), may hold values from -6 to 6
- query_rope: bfloat16 [1, 128, 64, 512], P(None, 'ep', None, 'ctx'), may hold values from -12 to 12
- key_latent: bfloat16 [1, 512, 512], P(None, 'ctx'), may hold values from -6 to 6
- key_rope: bfloat16 [1, 64, 512], P(None, None, 'ctx'), may hold values from -14 to 14
- output_grad: bfloat16 [1, 512, 128, 512], P(None, 'ctx', 'ep'), may hold values from -6 to 6
Outputs:
- attended: bfloat16 [1, 512, 128, 512], P(None, 'ctx', 'ep')
- query_latent_grad: bfloat16 [1, 512, 128, 512], P(None, 'ctx', 'ep')
- query_rope_grad: bfloat16 [1, 128, 64, 512], P(None, 'ep', None, 'ctx')
- key_latent_grad: bfloat16 [1, 512, 512], P(None, 'ctx')
- key_rope_grad: bfloat16 [1, 64, 512], P(None, None, 'ctx')
All inputs are finite; a program needn't handle non-finite values.
Results may differ from a plain program's by a relative error of at most 0.018.
Values may be sent and summed in bfloat16 or wider, within the bound.
No kernel may reach another device: no remote copies, remote signals or barrier semaphores. Data moves between devices by JAX's collectives and lax.ppermute only.
A program may use at most 64 MiB of HBM per device.

v0:
```python
import jax
import jax.numpy as jnp
from jax import lax
from jax.sharding import PartitionSpec as P

scale_factor = 192.0 ** (-0.5)


def causal_reduce_ctx(blocks, n_ctx):
    here = lax.axis_index("ctx")
    total = jnp.take(blocks, here, axis=0).astype(jnp.float32)
    for shift in range(1, n_ctx):
        sent = jnp.take(blocks, jnp.maximum(here - shift, 0), axis=0)
        got = lax.ppermute(sent, "ctx", [(i, i - shift) for i in range(shift, n_ctx)])
        total = total + got.astype(jnp.float32)
    return total


def halving_sum_ep(total, n_ep):
    if n_ep & n_ep - 1:
        return lax.psum(total.astype(jnp.bfloat16), "ep").astype(jnp.bfloat16)
    n_bits = n_ep.bit_length() - 1
    here = lax.axis_index("ep")
    rows, cols = total.shape
    parts = total.reshape((2,) * n_bits + (rows // n_ep, cols))
    for k in range(n_bits):
        axis = n_bits - 1 - k
        mine = here >> k & 1
        keep = jnp.take(parts, mine, axis=axis)
        sent = jnp.take(parts, 1 - mine, axis=axis).astype(jnp.bfloat16)
        got = lax.ppermute(sent, "ep", [(i, i ^ 1 << k) for i in range(n_ep)])
        parts = keep + got.astype(jnp.float32)
        n_left = n_bits - 1 - k
        parts = parts.reshape((2,) * n_left + (rows // n_ep, cols)) if n_left else parts
    whole = parts.astype(jnp.bfloat16)
    for k in reversed(range(n_bits)):
        mine = here >> k & 1
        got = lax.ppermute(whole, "ep", [(i, i ^ 1 << k) for i in range(n_ep)])
        low = jnp.where(mine == 0, whole, got)
        high = jnp.where(mine == 0, got, whole)
        whole = jnp.stack([low, high], axis=n_bits - 1 - k)
    return whole.reshape(rows, cols)


def body(query_latent, query_rope, key_latent, key_rope, output_grad):
    n_ctx = lax.axis_size("ctx")
    n_ep = lax.axis_size("ep")
    block_len = query_latent.shape[1]
    kvr = key_latent.shape[2]
    local_keys = jnp.concatenate([key_latent[0], key_rope[0].T], axis=1)
    whole_keys = lax.all_gather(local_keys, "ctx", axis=0, tiled=True)
    whole_latent = whole_keys[None, :, :kvr]
    whole_rope = whole_keys[:, kvr:].T[None]
    length = whole_latent.shape[1]
    offset = lax.axis_index("ctx") * block_len
    query_place = offset + jnp.arange(block_len, dtype=jnp.int32)
    allowed = jnp.arange(length, dtype=jnp.int32)[None, :] <= query_place[:, None]
    scores = jnp.einsum(
        "sthd,sjd->shtj", query_latent, whole_latent, preferred_element_type=jnp.float32
    )
    scores = scores + jnp.einsum(
        "shdt,sdj->shtj", query_rope, whole_rope, preferred_element_type=jnp.float32
    )
    scores = jnp.where(allowed, scores * scale_factor, jnp.float32(-1e30))
    row_max = jnp.max(scores, axis=-1, keepdims=True)
    powers = jnp.exp(scores - row_max)
    weights = powers / jnp.sum(powers, axis=-1, keepdims=True)
    rounded_weights = weights.astype(jnp.bfloat16)
    attended = jnp.einsum(
        "shtj,sjd->sthd", rounded_weights, whole_latent, preferred_element_type=jnp.float32
    ).astype(jnp.bfloat16)
    row_dots = jnp.einsum(
        "sthd,sthd->sht", output_grad, attended, preferred_element_type=jnp.float32
    )
    weight_grad = jnp.einsum(
        "sthd,sjd->shtj", output_grad, whole_latent, preferred_element_type=jnp.float32
    )
    score_grad = (weights * (weight_grad - row_dots[..., None])).astype(jnp.bfloat16)
    latent_qgrad = (
        scale_factor
        * jnp.einsum("shtj,sjd->sthd", score_grad, whole_latent, preferred_element_type=jnp.float32)
    ).astype(jnp.bfloat16)
    rope_qgrad = (
        scale_factor
        * jnp.einsum("shtj,sdj->shdt", score_grad, whole_rope, preferred_element_type=jnp.float32)
    ).astype(jnp.bfloat16)
    latent_term = scale_factor * jnp.einsum(
        "shtj,sthd->jd", score_grad, query_latent, preferred_element_type=jnp.float32
    )
    latent_term = latent_term + jnp.einsum(
        "shtj,sthd->jd", rounded_weights, output_grad, preferred_element_type=jnp.float32
    )
    rope_term = scale_factor * jnp.einsum(
        "shtj,shdt->jd", score_grad, query_rope, preferred_element_type=jnp.float32
    )
    terms = jnp.concatenate([latent_term, rope_term], axis=1).astype(jnp.bfloat16)
    total = causal_reduce_ctx(terms.reshape(n_ctx, block_len, -1), n_ctx)
    total = halving_sum_ep(total, n_ep)
    latent_kgrad = total[None, :, :kvr]
    rope_kgrad = total[:, kvr:].T[None]
    return (attended, latent_qgrad, rope_qgrad, latent_kgrad, rope_kgrad)


def solution(mesh):
    placed = (
        P(None, "ctx", "ep", None),
        P(None, "ep", None, "ctx"),
        P(None, "ctx", None),
        P(None, None, "ctx"),
        P(None, "ctx", "ep", None),
    )
    return jax.shard_map(
        body,
        mesh=mesh,
        in_specs=placed,
        out_specs=(
            P(None, "ctx", "ep", None),
            P(None, "ctx", "ep", None),
            P(None, "ep", None, "ctx"),
            P(None, "ctx", None),
            P(None, None, "ctx"),
        ),
        check_vma=False,
    )
```

profile of v0, /device:TPU:0, one launch (start us, length us, event | category | flops | bytes accessed | tf_op | source)
XLA Modules:
  0.0 101.1 jit_solution(4417357890290526066)
XLA Ops:
  0.6 0.0 copy-start
  0.6 1.0 copy.51
  1.6 0.9 pad_maximum_fusion
  2.6 9.3 %all_gather.3 = bf16[512,576]{1,0:T(8,128)(2,1)S(1)} all-gather(bf16[128,576]{1,0:T(8,128)(2,1)S(1)} %pad_maximum_fusion), channel_id=1, replica_groups=mesh['ctx'=4,'ep'=8] {'ctx'}, dimensions={0}, use_global_device_ids=true | all-gather | bytes 737280 | tf_op jit(solution)/shard_map/all_gather | solution.py:51
  11.9 0.1 iota_compare_fusion
  11.9 0.0 copy-done
  12.0 0.0 copy-start.4
  12.0 2.8 %fusion.23 = f32[512,128,16]{1,0,2:T(8,128)S(1)} fusion(bf16[128,16,512]{2,1,0:T(8,128)(2,1)S(1)} %bitcast.189, bf16[512,576]{1,0:T(8,128)(2,1)S(1)} %all_gather.3), kind=kOutput, calls=%fused_computation.27 | convolution fusion | flops 1073741824 | bytes 6815744 | tf_op jit(solution)/shard_map/sthd,sjd->shtj/dot_general | solution.py:58
  14.8 0.0 copy-done.4
  14.8 0.9 fusion.93
  15.7 0.0 copy-start.1
  15.7 0.6 fusion.5
  16.3 4.1 %bitcast_convert_fusion = (f32[16,128,512]{1,2,0:T(8,128)}, bf16[512,16,128]{2,0,1:T(8,128)(2,1)}) fusion(f32[16,128]{1,0:T(8,128)S(1)} %fusion.5, f32[1,16,128,512]{2,3,1,0:T(8,128)S(1)} %get-tuple-element.78, f32[16,128]{1,0:T(8,128)S(1)} %get-tuple-element.77, bf16[512,576]{1,0:T(8,128)(2,1)S(1)} %all_gather.3), kind=kOutput, calls=%fused_computation.18 | convolution fusion | flops 1078984704 | bytes 11026432 | tf_op jit(solution)/shard_map/shtj,sjd->sthd/dot_general | solution.py:69
  20.4 0.0 copy-done.1
  20.4 5.5 %copy.81 = f32[16,128,512]{2,0,1:T(8,128)} copy(f32[16,128,512]{1,2,0:T(8,128)} %get-tuple-element.79) | data formatting | bytes 8388608
  25.9 3.3 %multiply_reduce_fusion = f32[16,128]{0,1:T(8,128)S(1)} fusion(f32[16,128,512]{2,0,1:T(8,128)} %copy.81, bf16[1,128,16,512]{3,2,1,0:T(8,128)(2,1)} %param.17), kind=kLoop, calls=%fused_computation.6 | loop fusion | flops 3143680 | bytes 6299648
  29.3 0.1 copy.82
  29.3 0.0 copy-start.2
  29.3 0.0 copy-start.3
  29.3 6.8 %fusion.28 = f32[512,512]{1,0:T(8,128)} fusion(bf16[128,16,512]{2,1,0:T(8,128)(2,1)} %bitcast.191, f32[16,128]{1,0:T(8,128)S(1)} %fusion.5, f32[1,16,128,512]{2,3,1,0:T(8,128)} %copy-done.1, f32[16,128]{1,0:T(8,128)S(1)} %get-tuple-element.77), kind=kOutput, calls=%fused_computation.30 | convolution fusion | flops 1076887552 | bytes 7356416 | tf_op jit(solution)/shard_map/shtj,sthd->jd/dot_general | solution.py:90
  36.1 0.0 copy-done.2
  36.1 0.0 copy-done.3
  36.1 4.7 %fusion.1 = bf16[1,16,128,512]{2,3,1,0:T(8,128)(2,1)} fusion(f32[16,128]{1,0:T(8,128)S(1)} %copy.82, bf16[128,16,512]{2,1,0:T(8,128)(2,1)S(1)} %bitcast.192, f32[16,128]{1,0:T(8,128)S(1)} %fusion.5, f32[1,16,128,512]{2,3,1,0:T(8,128)S(1)} %copy-done.2, f32[16,128]{1,0:T(8,128)S(1)} %get-tuple-element.77, bf16[512,576]{1,0:T(8,128)(2,1)S(1)} %all_gather.3), kind=kOutput, calls=%fused_computation.2 | convolution fusion | flops 1078984704 | bytes 8937472 | tf_op jit(solution)/shard_map/sthd,sjd->shtj/dot_general | solution.py:75
  40.8 2.3 %fusion.69 = bf16[512,64]{0,1:T(8,128)(2,1)S(1)} fusion(bf16[1,16,128,512]{2,3,1,0:T(8,128)(2,1)} %fusion.1, bf16[1,16,64,128]{3,2,1,0:T(8,128)(2,1)S(1)} %copy-done.4), kind=kOutput, calls=%fused_computation.45 | convolution fusion | flops 134283264 | bytes 2424832 | tf_op jit(solution)/shard_map/shtj,shdt->jd/dot_general | solution.py:93
  43.1 4.4 %fusion.48 = bf16[512,512]{1,0:T(8,128)(2,1)S(1)} fusion(f32[512,512]{1,0:T(8,128)} %fusion.28, bf16[128,16,512]{2,1,0:T(8,128)(2,1)S(1)} %bitcast.190, bf16[1,16,128,512]{2,3,1,0:T(8,128)(2,1)} %fusion.1), kind=kOutput, calls=%fused_computation.34 | convolution fusion | flops 1074528256 | bytes 5767168 | tf_op jit(solution)/shard_map/shtj,sthd->jd/dot_general | solution.py:87
  47.6 0.1 copy.92
  47.7 0.8 fusion.82
  48.5 1.3 %collective-permute-start.2 = (bf16[128,576]{1,0:T(8,128)(2,1)}, bf16[128,576]{1,0:T(8,128)(2,1)}, u32[]{:S(2)}, u32[]{:S(2)}) collective-permute-start(bf16[128,576]{1,0:T(8,128)(2,1)} %get-tuple-element.70), channel_id=1, source_target_pairs={{24,0},{25,1},{26,2},{27,3},{28,4},{29,5},{30,6},{31,7}} | collective-permute-start | bytes 442376 | tf_op jit(solution)/shard_map/ppermute | solution.py:14
  49.8 1.3 %collective-permute-start.1 = (bf16[128,576]{1,0:T(8,128)(2,1)}, bf16[128,576]{1,0:T(8,128)(2,1)}, u32[]{:S(2)}, u32[]{:S(2)}) collective-permute-start(bf16[128,576]{1,0:T(8,128)(2,1)} %get-tuple-element.69), channel_id=1, source_target_pairs={{16,0},{24,8},{17,1},{25,9},{18,2},{26,10},{19,3},{27,11},{20,4},{... | collective-permute-start | bytes 442376 | tf_op jit(solution)/shard_map/ppermute | solution.py:14
  51.1 1.5 %collective-permute-start = (bf16[128,576]{1,0:T(8,128)(2,1)}, bf16[128,576]{1,0:T(8,128)(2,1)}, u32[]{:S(2)}, u32[]{:S(2)}) collective-permute-start(bf16[128,576]{1,0:T(8,128)(2,1)} %get-tuple-element.68), channel_id=1, source_target_pairs={{8,0},{16,8},{24,16},{9,1},{17,9},{25,17},{10,2},{18,10},{26,18},{... | collective-permute-start | bytes 442376 | tf_op jit(solution)/shard_map/ppermute | solution.py:14
  52.7 2.8 %collective-permute-done.2 = bf16[128,576]{1,0:T(8,128)(2,1)} collective-permute-done((bf16[128,576]{1,0:T(8,128)(2,1)}, bf16[128,576]{1,0:T(8,128)(2,1)}, u32[]{:S(2)}, u32[]{:S(2)}) %collective-permute-start.2) | collective-permute-done | bytes 147488 | tf_op jit(solution)/shard_map/ppermute | solution.py:14
  55.5 3.6 %collective-permute-done.1 = bf16[128,576]{1,0:T(8,128)(2,1)} collective-permute-done((bf16[128,576]{1,0:T(8,128)(2,1)}, bf16[128,576]{1,0:T(8,128)(2,1)}, u32[]{:S(2)}, u32[]{:S(2)}) %collective-permute-start.1) | collective-permute-done | bytes 147488 | tf_op jit(solution)/shard_map/ppermute | solution.py:14
  59.1 0.0 collective-permute-done
  59.1 1.2 %convert_add_fusion = f32[128,576]{1,0:T(8,128)S(1)} fusion(bf16[128,576]{1,0:T(8,128)(2,1)} %collective-permute-done.2, bf16[128,576]{1,0:T(8,128)(2,1)} %collective-permute-done.1, bf16[128,576]{1,0:T(8,128)(2,1)} %collective-permute-done, s32[]{:T(128)S(6)} %select_n.101, bf16[4,128,512]{2,1,0:T(8,128)(2,1)S(1)} %bitcast.195, ...), kind=kLoop, calls=%fused_computation.51 | loop fusion | flops 884736 | bytes 1327109 | tf_op jit(solution)/shard_map/add | solution.py:15
  60.2 0.0 copy-start.5
  60.2 0.7 copy-done.5
  61.0 1.6 %collective-permute-start.3 = (bf16[2,2,16,576]{3,2,1,0:T(8,128)(2,1)S(1)}, bf16[2,2,16,576]{3,2,1,0:T(8,128)(2,1)S(1)}, u32[]{:S(2)}, u32[]{:S(2)}) collective-permute-start(bf16[2,2,16,576]{3,2,1,0:T(8,128)(2,1)S(1)} %bitcast_convert_fusion.1), channel_id=1, source_target_pairs={{0,1},{1,0},{2,3},{3,2},{4,5},{5,4},{6,7},{7,6},{8,9},{9,8},{10,11... | collective-permute-start | bytes 221192 | tf_op jit(solution)/shard_map/ppermute | solution.py:31
  62.6 3.2 %collective-permute-done.3 = bf16[2,2,16,576]{3,2,1,0:T(8,128)(2,1)S(1)} collective-permute-done((bf16[2,2,16,576]{3,2,1,0:T(8,128)(2,1)S(1)}, bf16[2,2,16,576]{3,2,1,0:T(8,128)(2,1)S(1)}, u32[]{:S(2)}, u32[]{:S(2)}) %collective-permute-start.3) | collective-permute-done | bytes 73760 | tf_op jit(solution)/shard_map/ppermute | solution.py:31
  65.7 0.9 fusion.87
  66.7 1.6 %collective-permute-start.4 = (bf16[2,16,576]{2,1,0:T(8,128)(2,1)S(1)}, bf16[2,16,576]{2,1,0:T(8,128)(2,1)S(1)}, u32[]{:S(2)}, u32[]{:S(2)}) collective-permute-start(bf16[2,16,576]{2,1,0:T(8,128)(2,1)S(1)} %bitcast_convert_fusion.2), channel_id=1, source_target_pairs={{0,2},{1,3},{2,0},{3,1},{4,6},{5,7},{6,4},{7,5},{8,10},{9,11},{10,... | collective-permute-start | bytes 110600 | tf_op jit(solution)/shard_map/ppermute | solution.py:31
  68.3 2.4 %collective-permute-done.4 = bf16[2,16,576]{2,1,0:T(8,128)(2,1)S(1)} collective-permute-done((bf16[2,16,576]{2,1,0:T(8,128)(2,1)S(1)}, bf16[2,16,576]{2,1,0:T(8,128)(2,1)S(1)}, u32[]{:S(2)}, u32[]{:S(2)}) %collective-permute-start.4) | collective-permute-done | bytes 36896 | tf_op jit(solution)/shard_map/ppermute | solution.py:31
  70.8 2.7 %collective-permute-start.5 = (bf16[16,576]{1,0:T(8,128)(2,1)S(1)}, bf16[16,576]{1,0:T(8,128)(2,1)S(1)}, u32[]{:S(2)}, u32[]{:S(2)}) collective-permute-start(bf16[16,576]{1,0:T(8,128)(2,1)S(1)} %bitcast_convert_fusion.3), channel_id=1, source_target_pairs={{0,4},{1,5},{2,6},{3,7},{4,0},{5,1},{6,2},{7,3},{8,12},{9,13},{10,... | collective-permute-start | bytes 55304 | tf_op jit(solution)/shard_map/ppermute | solution.py:31
  73.5 2.1 %collective-permute-done.5 = bf16[16,576]{1,0:T(8,128)(2,1)S(1)} collective-permute-done((bf16[16,576]{1,0:T(8,128)(2,1)S(1)}, bf16[16,576]{1,0:T(8,128)(2,1)S(1)}, u32[]{:S(2)}, u32[]{:S(2)}) %collective-permute-start.5) | collective-permute-done | bytes 18464 | tf_op jit(solution)/shard_map/ppermute | solution.py:31
  75.6 2.7 %collective-permute-start.6 = (bf16[16,576]{1,0:T(8,128)(2,1)S(1)}, bf16[16,576]{1,0:T(8,128)(2,1)S(1)}, u32[]{:S(2)}, u32[]{:S(2)}) collective-permute-start(bf16[16,576]{1,0:T(8,128)(2,1)S(1)} %fusion.90), channel_id=1, source_target_pairs={{0,4},{1,5},{2,6},{3,7},{4,0},{5,1},{6,2},{7,3},{8,12},{9,13},{10,... | collective-permute-start | bytes 55304 | tf_op jit(solution)/shard_map/ppermute | solution.py:38
  78.2 2.2 %collective-permute-done.6 = bf16[16,576]{1,0:T(8,128)(2,1)S(1)} collective-permute-done((bf16[16,576]{1,0:T(8,128)(2,1)S(1)}, bf16[16,576]{1,0:T(8,128)(2,1)S(1)}, u32[]{:S(2)}, u32[]{:S(2)}) %collective-permute-start.6) | collective-permute-done | bytes 18464 | tf_op jit(solution)/shard_map/ppermute | solution.py:38
  80.4 1.5 %collective-permute-start.7 = (bf16[2,16,576]{2,1,0:T(8,128)(2,1)S(1)}, bf16[2,16,576]{2,1,0:T(8,128)(2,1)S(1)}, u32[]{:S(2)}, u32[]{:S(2)}) collective-permute-start(bf16[2,16,576]{2,1,0:T(8,128)(2,1)S(1)} %pad_maximum_fusion.3), channel_id=1, source_target_pairs={{0,2},{1,3},{2,0},{3,1},{4,6},{5,7},{6,4},{7,5},{8,10},{9,11},{10,... | collective-permute-start | bytes 110600 | tf_op jit(solution)/shard_map/ppermute | solution.py:38
  82.0 4.2 %fusion.25 = bf16[1,128,16,512]{1,3,2,0:T(8,128)(2,1)} fusion(bf16[1,16,128,512]{2,3,1,0:T(8,128)(2,1)} %fusion.1, bf16[512,576]{1,0:T(8,128)(2,1)S(1)} %all_gather.3), kind=kOutput, calls=%fused_computation.29 | convolution fusion | flops 1075838976 | bytes 4718592 | tf_op jit(solution)/shard_map/shtj,sjd->sthd/dot_general | solution.py:81
  86.2 0.0 collective-permute-done.7
  86.2 1.6 %collective-permute-start.8 = (bf16[2,2,16,576]{3,2,0,1:T(8,128)(2,1)S(1)}, bf16[2,2,16,576]{3,2,0,1:T(8,128)(2,1)S(1)}, u32[]{:S(2)}, u32[]{:S(2)}) collective-permute-start(bf16[2,2,16,576]{3,2,0,1:T(8,128)(2,1)S(1)} %pad_maximum_fusion.2), channel_id=1, source_target_pairs={{0,1},{1,0},{2,3},{3,2},{4,5},{5,4},{6,7},{7,6},{8,9},{9,8},{10,11... | collective-permute-start | bytes 221192 | tf_op jit(solution)/shard_map/ppermute | solution.py:38
  87.8 2.8 %fusion.60 = bf16[1,16,64,128]{3,2,1,0:T(8,128)(2,1)} fusion(bf16[1,16,128,512]{2,3,1,0:T(8,128)(2,1)} %fusion.1, bf16[512,576]{1,0:T(8,128)(2,1)S(1)} %all_gather.3), kind=kOutput, calls=%fused_computation.42 | convolution fusion | flops 134479872 | bytes 2490368 | tf_op jit(solution)/shard_map/shtj,sdj->shdt/dot_general | solution.py:85
  90.6 4.5 %copy.70 = bf16[1,128,16,512]{3,2,1,0:T(8,128)(2,1)} copy(bf16[1,128,16,512]{1,3,2,0:T(8,128)(2,1)} %bitcast.193) | data formatting | bytes 4194304
  95.1 4.5 %copy.71 = bf16[1,128,16,512]{3,2,1,0:T(8,128)(2,1)} copy(bf16[1,128,16,512]{1,3,2,0:T(8,128)(2,1)} %fusion.25) | data formatting | bytes 4194304
  99.6 0.0 collective-permute-done.8
  99.7 0.7 slice_bitcast_fusion.5
  100.4 0.7 copy.72
  (14 shorter events, 0.2 us)
Async XLA Ops:
  0.6 11.3 %copy-start = (bf16[1,128,16,512]{3,2,1,0:T(8,128)(2,1)S(1)}, bf16[1,128,16,512]{3,2,1,0:T(8,128)(2,1)}, u32[]{:S(2)}) copy-start(bf16[1,128,16,512]{3,2,1,0:T(8,128)(2,1)} %param.13) | copy-start | bytes 6291460
  12.0 2.8 %copy-start.4 = (bf16[1,16,64,128]{3,2,1,0:T(8,128)(2,1)S(1)}, bf16[1,16,64,128]{3,2,1,0:T(8,128)(2,1)}, u32[]{:S(2)}) copy-start(bf16[1,16,64,128]{3,2,1,0:T(8,128)(2,1)} %param.14) | copy-start | bytes 786436
  15.7 4.7 %copy-start.1 = (f32[1,16,128,512]{2,3,1,0:T(8,128)}, f32[1,16,128,512]{2,3,1,0:T(8,128)S(1)}, u32[]{:S(2)}) copy-start(f32[1,16,128,512]{2,3,1,0:T(8,128)S(1)} %get-tuple-element.78) | copy-start | bytes 12582916
  29.3 6.8 %copy-start.2 = (f32[1,16,128,512]{2,3,1,0:T(8,128)S(1)}, f32[1,16,128,512]{2,3,1,0:T(8,128)}, u32[]{:S(2)}) copy-start(f32[1,16,128,512]{2,3,1,0:T(8,128)} %copy-done.1) | copy-start | bytes 12582916
  29.3 6.8 %copy-start.3 = (bf16[1,128,16,512]{3,2,1,0:T(8,128)(2,1)S(1)}, bf16[1,128,16,512]{3,2,1,0:T(8,128)(2,1)}, u32[]{:S(2)}) copy-start(bf16[1,128,16,512]{3,2,1,0:T(8,128)(2,1)} %param.17) | copy-start | bytes 6291460
  48.5 6.9 %collective-permute-start.2 = (bf16[128,576]{1,0:T(8,128)(2,1)}, bf16[128,576]{1,0:T(8,128)(2,1)}, u32[]{:S(2)}, u32[]{:S(2)}) collective-permute-start(bf16[128,576]{1,0:T(8,128)(2,1)} %get-tuple-element.70), channel_id=1, source_target_pairs={{24,0},{25,1},{26,2},{27,3},{28,4},{29,5},{30,6},{31,7}} | collective-permute-start | bytes 442376 | tf_op jit(solution)/shard_map/ppermute | solution.py:14
  49.8 9.2 %collective-permute-start.1 = (bf16[128,576]{1,0:T(8,128)(2,1)}, bf16[128,576]{1,0:T(8,128)(2,1)}, u32[]{:S(2)}, u32[]{:S(2)}) collective-permute-start(bf16[128,576]{1,0:T(8,128)(2,1)} %get-tuple-element.69), channel_id=1, source_target_pairs={{16,0},{24,8},{17,1},{25,9},{18,2},{26,10},{19,3},{27,11},{20,4},{... | collective-permute-start | bytes 442376 | tf_op jit(solution)/shard_map/ppermute | solution.py:14
  51.1 7.9 %collective-permute-start = (bf16[128,576]{1,0:T(8,128)(2,1)}, bf16[128,576]{1,0:T(8,128)(2,1)}, u32[]{:S(2)}, u32[]{:S(2)}) collective-permute-start(bf16[128,576]{1,0:T(8,128)(2,1)} %get-tuple-element.68), channel_id=1, source_target_pairs={{8,0},{16,8},{24,16},{9,1},{17,9},{25,17},{10,2},{18,10},{26,18},{... | collective-permute-start | bytes 442376 | tf_op jit(solution)/shard_map/ppermute | solution.py:14
  60.2 0.7 copy-start.5
  61.0 4.8 %collective-permute-start.3 = (bf16[2,2,16,576]{3,2,1,0:T(8,128)(2,1)S(1)}, bf16[2,2,16,576]{3,2,1,0:T(8,128)(2,1)S(1)}, u32[]{:S(2)}, u32[]{:S(2)}) collective-permute-start(bf16[2,2,16,576]{3,2,1,0:T(8,128)(2,1)S(1)} %bitcast_convert_fusion.1), channel_id=1, source_target_pairs={{0,1},{1,0},{2,3},{3,2},{4,5},{5,4},{6,7},{7,6},{8,9},{9,8},{10,11... | collective-permute-start | bytes 221192 | tf_op jit(solution)/shard_map/ppermute | solution.py:31
  66.7 4.1 %collective-permute-start.4 = (bf16[2,16,576]{2,1,0:T(8,128)(2,1)S(1)}, bf16[2,16,576]{2,1,0:T(8,128)(2,1)S(1)}, u32[]{:S(2)}, u32[]{:S(2)}) collective-permute-start(bf16[2,16,576]{2,1,0:T(8,128)(2,1)S(1)} %bitcast_convert_fusion.2), channel_id=1, source_target_pairs={{0,2},{1,3},{2,0},{3,1},{4,6},{5,7},{6,4},{7,5},{8,10},{9,11},{10,... | collective-permute-start | bytes 110600 | tf_op jit(solution)/shard_map/ppermute | solution.py:31
  70.8 4.7 %collective-permute-start.5 = (bf16[16,576]{1,0:T(8,128)(2,1)S(1)}, bf16[16,576]{1,0:T(8,128)(2,1)S(1)}, u32[]{:S(2)}, u32[]{:S(2)}) collective-permute-start(bf16[16,576]{1,0:T(8,128)(2,1)S(1)} %bitcast_convert_fusion.3), channel_id=1, source_target_pairs={{0,4},{1,5},{2,6},{3,7},{4,0},{5,1},{6,2},{7,3},{8,12},{9,13},{10,... | collective-permute-start | bytes 55304 | tf_op jit(solution)/shard_map/ppermute | solution.py:31
  75.6 4.9 %collective-permute-start.6 = (bf16[16,576]{1,0:T(8,128)(2,1)S(1)}, bf16[16,576]{1,0:T(8,128)(2,1)S(1)}, u32[]{:S(2)}, u32[]{:S(2)}) collective-permute-start(bf16[16,576]{1,0:T(8,128)(2,1)S(1)} %fusion.90), channel_id=1, source_target_pairs={{0,4},{1,5},{2,6},{3,7},{4,0},{5,1},{6,2},{7,3},{8,12},{9,13},{10,... | collective-permute-start | bytes 55304 | tf_op jit(solution)/shard_map/ppermute | solution.py:38
  80.4 5.7 %collective-permute-start.7 = (bf16[2,16,576]{2,1,0:T(8,128)(2,1)S(1)}, bf16[2,16,576]{2,1,0:T(8,128)(2,1)S(1)}, u32[]{:S(2)}, u32[]{:S(2)}) collective-permute-start(bf16[2,16,576]{2,1,0:T(8,128)(2,1)S(1)} %pad_maximum_fusion.3), channel_id=1, source_target_pairs={{0,2},{1,3},{2,0},{3,1},{4,6},{5,7},{6,4},{7,5},{8,10},{9,11},{10,... | collective-permute-start | bytes 110600 | tf_op jit(solution)/shard_map/ppermute | solution.py:38
  86.2 13.4 %collective-permute-start.8 = (bf16[2,2,16,576]{3,2,0,1:T(8,128)(2,1)S(1)}, bf16[2,2,16,576]{3,2,0,1:T(8,128)(2,1)S(1)}, u32[]{:S(2)}, u32[]{:S(2)}) collective-permute-start(bf16[2,2,16,576]{3,2,0,1:T(8,128)(2,1)S(1)} %pad_maximum_fusion.2), channel_id=1, source_target_pairs={{0,1},{1,0},{2,3},{3,2},{4,5},{5,4},{6,7},{7,6},{8,9},{9,8},{10,11... | collective-permute-start | bytes 221192 | tf_op jit(solution)/shard_map/ppermute | solution.py:38
where the time goes:
time: 102 us; the launch traced here: 101 us
  matrix products  33.1 us (32%)
  local copies, waits for them, and re-layouts  17.7 us (17%)
  waiting for transfers between devices  16.3 us (16%)
  starting transfers between devices  15.8 us (15%)
  blocking collectives  9.33 us (9%)
  other arithmetic  8.02 us (8%)
    unnamed x17, local copies, waits for them, and re-layouts  16.9 us
    all_gather x1, blocking collectives, body(): whole_keys = lax.all_gather(local_keys, 'ctx', axis=0, tiled=True)  9.33 us
    ppermute x3, waiting for transfers between devices, halving_sum_ep(): got = lax.ppermute(sent, 'ep', [(i, i ^ 1 << k) for i in range(n_ep)])  7.69 us
    dot_general x1, matrix products, body(): jnp.einsum('shtj,sthd->jd', rounded_weights, output_grad, preferred_eleme...  6.77 us
    ppermute x3, waiting for transfers between devices, causal_reduce_ctx(): lax.ppermute(sent, 'ctx', [(i, i - shift) for i in range(shift, n_ctx)])  6.4 us
    ppermute x3, starting transfers between devices, halving_sum_ep(): got = lax.ppermute(sent, 'ep', [(i, i ^ 1 << k) for i in range(n_ep)])  5.88 us
    ppermute x3, starting transfers between devices, halving_sum_ep(): got = lax.ppermute(whole, 'ep', [(i, i ^ 1 << k) for i in range(n_ep)])  5.79 us
    dot_general x1, matrix products, body(): jnp.einsum('sthd,sjd->shtj', output_grad, whole_latent, preferred_element...  4.7 us
  transfers between devices with their start and end apart: 9, of which 6 were waited for; matrix products, arithmetic and copies ran while one was open for 16% of the time, Pallas kernels for 0%

commit v1 on v0

--- a/solution.py
+++ b/solution.py
@@ -1,9 +1,34 @@
+import functools
 import jax
 import jax.numpy as jnp
 from jax import lax
 from jax.sharding import PartitionSpec as P
+from jax.lax import axis_index, axis_size, ppermute
 
 scale_factor = 192.0 ** (-0.5)
+
+
+def play_figure(x0, across):
+    left_arr = axis_size(across)
+    after, res, main = (left_arr, axis_index(across), x0.shape[0])
+    by_rank = [dev * after if ii == 0 else dev for ii, dev in enumerate(x0.shape)]
+    q_next = jnp.zeros(by_rank, x0.dtype)
+    clean = lax.dynamic_update_slice_in_dim(q_next, x0, res * main, axis=0)
+    tile_out = aux = x0
+    for c in range(1, after // 2 + 1):
+        tile_out = ppermute(
+            tile_out, axis_name=across, perm=[(ii, (ii + 1) % after) for ii in range(after)]
+        )
+        clean = lax.dynamic_update_slice_in_dim(clean, tile_out, (res - c) % after * main, axis=0)
+        if 2 * c < after:
+            aux = ppermute(
+                aux, axis_name=across, perm=[(ii, (ii - 1) % after) for ii in range(after)]
+            )
+            clean = lax.dynamic_update_slice_in_dim(clean, aux, (res + c) % after * main, axis=0)
+    return clean
+
+
+try_all_skins = functools.partial(play_figure, across="ctx")
 
 
 def causal_reduce_ctx(blocks, n_ctx):
@@ -48,7 +73,7 @@
     block_len = query_latent.shape[1]
     kvr = key_latent.shape[2]
     local_keys = jnp.concatenate([key_latent[0], key_rope[0].T], axis=1)
-    whole_keys = lax.all_gather(local_keys, "ctx", axis=0, tiled=True)
+    whole_keys = try_all_skins(local_keys)
     whole_latent = whole_keys[None, :, :kvr]
     whole_rope = whole_keys[:, kvr:].T[None]
     length = whole_latent.shape[1]

time: 102 us -> 96.5 us (0.946)
  blocking collectives: 9.33 us -> 0 us
  matrix products: 33.1 us -> 25.7 us
  waiting for transfers between devices: 16.3 us -> 23 us
  starting transfers between devices: 15.8 us -> 19.8 us
    all_gather x1 -> x0, blocking collectives: 9.33 us -> none  [body(): whole_keys = lax.all_gather(local_keys, 'ctx', axis=0, tiled=True)]
    ppermute x0 -> x3, waiting for transfers between devices: none -> 5.89 us  [the longest x2 5.89 us: play_figure(): ppermute(tile_out, axis_name=across, perm=[(ii, (ii + 1) % after) for ii...]
    ppermute x0 -> x3, starting transfers between devices: none -> 4.1 us  [the longest x2 2.11 us: play_figure(): ppermute(tile_out, axis_name=across, perm=[(ii, (ii + 1) % after) for ii...]
    dot_general x1, matrix products: 4.44 us -> 2.57 us  [body(): jnp.einsum('shtj,sthd->jd', score_grad, query_latent, preferred_element_t...]
    dot_general x1, matrix products: 2.8 us -> 1.21 us  [body(): jnp.einsum('shtj,sdj->shdt', score_grad, whole_rope, preferred_element_ty...]
    dot_general x1, matrix products: 2.34 us -> 0.75 us  [body(): jnp.einsum('shtj,shdt->jd', score_grad, query_rope, preferred_element_typ...]
    dot_general x1, matrix products: 4.7 us -> 3.37 us  [body(): jnp.einsum('sthd,sjd->shtj', output_grad, whole_latent, preferred_element...]
    unnamed x17 -> x21, local copies, waits for them, and re-layouts: 16.9 us -> 17.5 us
  transfers between devices with their start and end apart: 9 -> 12, of which waited for: 6 -> 8; matrix products, arithmetic and copies ran while one was open for 16% -> 15% of each run, Pallas kernels for 0% -> 0%
where the time goes in v1:
time: 96.5 us; the launch traced here: 96 us
  matrix products  25.7 us (27%)
  waiting for transfers between devices  23 us (24%)
  starting transfers between devices  19.8 us (21%)
  local copies, waits for them, and re-layouts  18.4 us (19%)
  other arithmetic  8.05 us (8%)
  between operations  0.97 us (1%)
    unnamed x21, local copies, waits for them, and re-layouts  17.5 us
    ppermute x3, waiting for transfers between devices, halving_sum_ep(): got = lax.ppermute(sent, 'ep', [(i, i ^ 1 << k) for i in range(n_ep)])  7.76 us
    ppermute x3, waiting for transfers between devices, causal_reduce_ctx(): lax.ppermute(sent, 'ctx', [(i, i - shift) for i in range(shift, n_ctx)])  7.11 us
    ppermute x3, starting transfers between devices, halving_sum_ep(): got = lax.ppermute(sent, 'ep', [(i, i ^ 1 << k) for i in range(n_ep)])  5.91 us
    ppermute x2, waiting for transfers between devices, play_figure(): ppermute(tile_out, axis_name=across, perm=[(ii, (ii + 1) % after) for ii...  5.89 us
    dot_general x1, matrix products, body(): jnp.einsum('shtj,sthd->jd', rounded_weights, output_grad, preferred_eleme...  5.8 us
    ppermute x3, starting transfers between devices, halving_sum_ep(): got = lax.ppermute(whole, 'ep', [(i, i ^ 1 << k) for i in range(n_ep)])  5.74 us
    dot_general x1, matrix products, body(): jnp.einsum('shtj,sjd->sthd', score_grad, whole_latent, preferred_element_...  4.21 us
  transfers between devices with their start and end apart: 12, of which 8 were waited for; matrix products, arithmetic and copies ran while one was open for 15% of the time, Pallas kernels for 0%

profile of v1, /device:TPU:0, one launch (start us, length us, event | category | flops | bytes accessed | tf_op | source)
XLA Modules:
  0.0 96.0 jit_solution(1523778104082245231)
XLA Ops:
  0.6 0.0 copy-start
  0.6 1.0 %copy.51 = bf16[1,64,128]{1,2,0:T(8,128)(2,1)S(1)} copy(bf16[1,64,128]{2,1,0:T(8,128)(2,1)} %param.16) | data formatting | bytes 32768 | tf_op args[3]
  1.6 0.1 broadcast_in_dim.60
  1.7 0.9 pad_maximum_fusion
  2.6 0.5 collective-permute-start
  3.1 2.0 %collective-permute-start.1 = (bf16[128,576]{1,0:T(8,128)(2,1)S(1)}, bf16[128,576]{1,0:T(8,128)(2,1)S(1)}, u32[]{:S(2)}, u32[]{:S(2)}) collective-permute-start(bf16[128,576]{1,0:T(8,128)(2,1)S(1)} %get-tuple-element.73), channel_id=1, source_target_pairs={{0,24},{8,0},{16,8},{24,16},{1,25},{9,1},{17,9},{25,17},{2,26},{10... | collective-permute-start | bytes 442376 | tf_op jit(solution)/shard_map/ppermute | solution.py:24
  5.1 0.1 iota_compare_fusion
  5.3 2.8 %collective-permute-done = bf16[128,576]{1,0:T(8,128)(2,1)S(1)} collective-permute-done((bf16[128,576]{1,0:T(8,128)(2,1)S(1)}, bf16[128,576]{1,0:T(8,128)(2,1)S(1)}, u32[]{:S(2)}, u32[]{:S(2)}) %collective-permute-start) | collective-permute-done | bytes 147488 | tf_op jit(solution)/shard_map/ppermute | solution.py:19
  8.1 1.6 %collective-permute-start.2 = (bf16[128,576]{1,0:T(8,128)(2,1)S(1)}, bf16[128,576]{1,0:T(8,128)(2,1)S(1)}, u32[]{:S(2)}, u32[]{:S(2)}) collective-permute-start(bf16[128,576]{1,0:T(8,128)(2,1)S(1)} %collective-permute-done), channel_id=1, source_target_pairs={{0,8},{8,16},{16,24},{24,0},{1,9},{9,17},{17,25},{25,1},{2,10},{10... | collective-permute-start | bytes 442376 | tf_op jit(solution)/shard_map/ppermute | solution.py:19
  9.7 0.0 collective-permute-done.1
  9.8 3.1 %collective-permute-done.2 = bf16[128,576]{1,0:T(8,128)(2,1)S(1)} collective-permute-done((bf16[128,576]{1,0:T(8,128)(2,1)S(1)}, bf16[128,576]{1,0:T(8,128)(2,1)S(1)}, u32[]{:S(2)}, u32[]{:S(2)}) %collective-permute-start.2) | collective-permute-done | bytes 147488 | tf_op jit(solution)/shard_map/ppermute | solution.py:19
  12.8 0.0 copy-done
  12.9 0.0 copy-start.6
  12.9 2.8 %fusion.23 = f32[512,128,16]{1,0,2:T(8,128)S(1)} fusion(bf16[128,16,512]{2,1,0:T(8,128)(2,1)S(1)} %bitcast.189, bf16[512,576]{1,0:T(8,128)(2,1)S(1)} %constant_dynamic-update-slice_fusion), kind=kOutput, calls=%fused_computation.27 | convolution fusion | flops 1073741824 | bytes 6815744 | tf_op jit(solution)/shard_map/sthd,sjd->shtj/dot_general | solution.py:83
  15.7 0.0 copy-done.6
  15.7 0.9 fusion.93
  16.6 0.0 copy-start.1
  16.6 0.6 fusion.5
  17.2 4.1 %bitcast_convert_fusion = (f32[16,128,512]{1,2,0:T(8,128)}, bf16[512,16,128]{2,0,1:T(8,128)(2,1)}) fusion(f32[16,128]{1,0:T(8,128)S(1)} %fusion.5, f32[1,16,128,512]{2,3,1,0:T(8,128)S(1)} %get-tuple-element.80, f32[16,128]{1,0:T(8,128)S(1)} %get-tuple-element.79, bf16[512,576]{1,0:T(8,128)(2,1)S(1)} %constant_dynamic-update-slice_fusion), kind=kOutput, calls=%fused_computation.18 | convolution fusion | flops 1078984704 | bytes 11026432 | tf_op jit(solution)/shard_map/shtj,sjd->sthd/dot_general | solution.py:94
  21.3 0.0 copy-done.1
  21.3 5.5 %copy.81 = f32[16,128,512]{2,0,1:T(8,128)} copy(f32[16,128,512]{1,2,0:T(8,128)} %get-tuple-element.81) | data formatting | bytes 8388608
  26.8 3.3 %multiply_reduce_fusion = f32[16,128]{0,1:T(8,128)S(1)} fusion(f32[16,128,512]{2,0,1:T(8,128)} %copy.81, bf16[1,128,16,512]{3,2,1,0:T(8,128)(2,1)} %param.17), kind=kLoop, calls=%fused_computation.6 | loop fusion | flops 3143680 | bytes 6299648
  30.2 0.1 copy.82
  30.2 0.0 copy-start.2
  30.2 0.0 copy-start.5
  30.2 5.8 %fusion.28 = f32[512,512]{1,0:T(8,128)S(1)} fusion(bf16[128,16,512]{2,1,0:T(8,128)(2,1)} %bitcast.191, f32[16,128]{1,0:T(8,128)S(1)} %fusion.5, f32[1,16,128,512]{2,3,1,0:T(8,128)} %copy-done.1, f32[16,128]{1,0:T(8,128)S(1)} %get-tuple-element.79), kind=kOutput, calls=%fused_computation.30 | convolution fusion | flops 1076887552 | bytes 7356416 | tf_op jit(solution)/shard_map/shtj,sthd->jd/dot_general | solution.py:115
  36.0 0.0 copy-done.2
  36.0 0.0 copy-done.5
  36.0 3.4 %fusion.1 = bf16[1,16,128,512]{2,3,1,0:T(8,128)(2,1)S(1)} fusion(f32[16,128]{1,0:T(8,128)S(1)} %copy.82, bf16[128,16,512]{2,1,0:T(8,128)(2,1)S(1)} %bitcast.192, f32[16,128]{1,0:T(8,128)S(1)} %fusion.5, f32[1,16,128,512]{2,3,1,0:T(8,128)S(1)} %copy-done.2, f32[16,128]{1,0:T(8,128)S(1)} %get-tuple-element.79, ...), kind=kOutput, calls=%fused_computation.2 | convolution fusion | flops 1078984704 | bytes 8937472 | tf_op jit(solution)/shard_map/sthd,sjd->shtj/dot_general | solution.py:100
  39.4 0.0 copy-start.3
  39.4 0.8 fusion.69
  40.2 0.6 copy-done.3
  40.7 2.6 %fusion.48 = bf16[512,512]{1,0:T(8,128)(2,1)S(1)} fusion(f32[512,512]{1,0:T(8,128)S(1)} %fusion.28, bf16[128,16,512]{2,1,0:T(8,128)(2,1)S(1)} %bitcast.190, bf16[1,16,128,512]{2,3,1,0:T(8,128)(2,1)S(1)} %fusion.1), kind=kOutput, calls=%fused_computation.34 | convolution fusion | flops 1074528256 | bytes 5767168 | tf_op jit(solution)/shard_map/shtj,sthd->jd/dot_general | solution.py:112
  43.3 0.1 copy.92
  43.4 0.8 fusion.82
  44.3 1.3 %collective-permute-start.5 = (bf16[128,576]{1,0:T(8,128)(2,1)}, bf16[128,576]{1,0:T(8,128)(2,1)}, u32[]{:S(2)}, u32[]{:S(2)}) collective-permute-start(bf16[128,576]{1,0:T(8,128)(2,1)} %get-tuple-element.70), channel_id=1, source_target_pairs={{24,0},{25,1},{26,2},{27,3},{28,4},{29,5},{30,6},{31,7}} | collective-permute-start | bytes 442376 | tf_op jit(solution)/shard_map/ppermute | solution.py:39
  45.6 1.3 %collective-permute-start.4 = (bf16[128,576]{1,0:T(8,128)(2,1)}, bf16[128,576]{1,0:T(8,128)(2,1)}, u32[]{:S(2)}, u32[]{:S(2)}) collective-permute-start(bf16[128,576]{1,0:T(8,128)(2,1)} %get-tuple-element.69), channel_id=1, source_target_pairs={{16,0},{24,8},{17,1},{25,9},{18,2},{26,10},{19,3},{27,11},{20,4},{... | collective-permute-start | bytes 442376 | tf_op jit(solution)/shard_map/ppermute | solution.py:39
  46.9 1.5 %collective-permute-start.3 = (bf16[128,576]{1,0:T(8,128)(2,1)}, bf16[128,576]{1,0:T(8,128)(2,1)}, u32[]{:S(2)}, u32[]{:S(2)}) collective-permute-start(bf16[128,576]{1,0:T(8,128)(2,1)} %get-tuple-element.68), channel_id=1, source_target_pairs={{8,0},{16,8},{24,16},{9,1},{17,9},{25,17},{10,2},{18,10},{26,18},{... | collective-permute-start | bytes 442376 | tf_op jit(solution)/shard_map/ppermute | solution.py:39
  48.4 2.8 %collective-permute-done.5 = bf16[128,576]{1,0:T(8,128)(2,1)} collective-permute-done((bf16[128,576]{1,0:T(8,128)(2,1)}, bf16[128,576]{1,0:T(8,128)(2,1)}, u32[]{:S(2)}, u32[]{:S(2)}) %collective-permute-start.5) | collective-permute-done | bytes 147488 | tf_op jit(solution)/shard_map/ppermute | solution.py:39
  51.2 4.3 %collective-permute-done.4 = bf16[128,576]{1,0:T(8,128)(2,1)} collective-permute-done((bf16[128,576]{1,0:T(8,128)(2,1)}, bf16[128,576]{1,0:T(8,128)(2,1)}, u32[]{:S(2)}, u32[]{:S(2)}) %collective-permute-start.4) | collective-permute-done | bytes 147488 | tf_op jit(solution)/shard_map/ppermute | solution.py:39
  55.5 0.0 collective-permute-done.3
  55.5 1.2 %convert_add_fusion = f32[128,576]{1,0:T(8,128)S(1)} fusion(bf16[128,576]{1,0:T(8,128)(2,1)} %collective-permute-done.5, bf16[128,576]{1,0:T(8,128)(2,1)} %collective-permute-done.4, bf16[128,576]{1,0:T(8,128)(2,1)} %collective-permute-done.3, s32[]{:T(128)S(6)} %select_n.134, bf16[4,128,512]{2,1,0:T(8,128)(2,1)S(1)} %bitcast.195, ...), kind=kLoop, calls=%fused_computation.51 | loop fusion | flops 884736 | bytes 1327109 | tf_op jit(solution)/shard_map/add | solution.py:40
  56.7 0.0 copy-start.7
  56.7 0.7 copy-done.7
  57.4 1.7 %collective-permute-start.6 = (bf16[2,2,16,576]{3,2,1,0:T(8,128)(2,1)S(1)}, bf16[2,2,16,576]{3,2,1,0:T(8,128)(2,1)S(1)}, u32[]{:S(2)}, u32[]{:S(2)}) collective-permute-start(bf16[2,2,16,576]{3,2,1,0:T(8,128)(2,1)S(1)} %bitcast_convert_fusion.1), channel_id=1, source_target_pairs={{0,1},{1,0},{2,3},{3,2},{4,5},{5,4},{6,7},{7,6},{8,9},{9,8},{10,11... | collective-permute-start | bytes 221192 | tf_op jit(solution)/shard_map/ppermute | solution.py:56
  59.1 3.2 %collective-permute-done.6 = bf16[2,2,16,576]{3,2,1,0:T(8,128)(2,1)S(1)} collective-permute-done((bf16[2,2,16,576]{3,2,1,0:T(8,128)(2,1)S(1)}, bf16[2,2,16,576]{3,2,1,0:T(8,128)(2,1)S(1)}, u32[]{:S(2)}, u32[]{:S(2)}) %collective-permute-start.6) | collective-permute-done | bytes 73760 | tf_op jit(solution)/shard_map/ppermute | solution.py:56
  62.3 0.9 fusion.87
  63.2 1.6 %collective-permute-start.7 = (bf16[2,16,576]{2,1,0:T(8,128)(2,1)S(1)}, bf16[2,16,576]{2,1,0:T(8,128)(2,1)S(1)}, u32[]{:S(2)}, u32[]{:S(2)}) collective-permute-start(bf16[2,16,576]{2,1,0:T(8,128)(2,1)S(1)} %bitcast_convert_fusion.2), channel_id=1, source_target_pairs={{0,2},{1,3},{2,0},{3,1},{4,6},{5,7},{6,4},{7,5},{8,10},{9,11},{10,... | collective-permute-start | bytes 110600 | tf_op jit(solution)/shard_map/ppermute | solution.py:56
  64.8 2.5 %collective-permute-done.7 = bf16[2,16,576]{2,1,0:T(8,128)(2,1)S(1)} collective-permute-done((bf16[2,16,576]{2,1,0:T(8,128)(2,1)S(1)}, bf16[2,16,576]{2,1,0:T(8,128)(2,1)S(1)}, u32[]{:S(2)}, u32[]{:S(2)}) %collective-permute-start.7) | collective-permute-done | bytes 36896 | tf_op jit(solution)/shard_map/ppermute | solution.py:56
  67.3 2.6 %collective-permute-start.8 = (bf16[16,576]{1,0:T(8,128)(2,1)S(1)}, bf16[16,576]{1,0:T(8,128)(2,1)S(1)}, u32[]{:S(2)}, u32[]{:S(2)}) collective-permute-start(bf16[16,576]{1,0:T(8,128)(2,1)S(1)} %bitcast_convert_fusion.3), channel_id=1, source_target_pairs={{0,4},{1,5},{2,6},{3,7},{4,0},{5,1},{6,2},{7,3},{8,12},{9,13},{10,... | collective-permute-start | bytes 55304 | tf_op jit(solution)/shard_map/ppermute | solution.py:56
  70.0 2.1 %collective-permute-done.8 = bf16[16,576]{1,0:T(8,128)(2,1)S(1)} collective-permute-done((bf16[16,576]{1,0:T(8,128)(2,1)S(1)}, bf16[16,576]{1,0:T(8,128)(2,1)S(1)}, u32[]{:S(2)}, u32[]{:S(2)}) %collective-permute-start.8) | collective-permute-done | bytes 18464 | tf_op jit(solution)/shard_map/ppermute | solution.py:56
  72.1 2.6 %collective-permute-start.9 = (bf16[16,576]{1,0:T(8,128)(2,1)S(1)}, bf16[16,576]{1,0:T(8,128)(2,1)S(1)}, u32[]{:S(2)}, u32[]{:S(2)}) collective-permute-start(bf16[16,576]{1,0:T(8,128)(2,1)S(1)} %fusion.90), channel_id=1, source_target_pairs={{0,4},{1,5},{2,6},{3,7},{4,0},{5,1},{6,2},{7,3},{8,12},{9,13},{10,... | collective-permute-start | bytes 55304 | tf_op jit(solution)/shard_map/ppermute | solution.py:63
  74.7 2.2 %collective-permute-done.9 = bf16[16,576]{1,0:T(8,128)(2,1)S(1)} collective-permute-done((bf16[16,576]{1,0:T(8,128)(2,1)S(1)}, bf16[16,576]{1,0:T(8,128)(2,1)S(1)}, u32[]{:S(2)}, u32[]{:S(2)}) %collective-permute-start.9) | collective-permute-done | bytes 18464 | tf_op jit(solution)/shard_map/ppermute | solution.py:63
  77.0 1.5 %collective-permute-start.10 = (bf16[2,16,576]{2,1,0:T(8,128)(2,1)S(1)}, bf16[2,16,576]{2,1,0:T(8,128)(2,1)S(1)}, u32[]{:S(2)}, u32[]{:S(2)}) collective-permute-start(bf16[2,16,576]{2,1,0:T(8,128)(2,1)S(1)} %pad_maximum_fusion.3), channel_id=1, source_target_pairs={{0,2},{1,3},{2,0},{3,1},{4,6},{5,7},{6,4},{7,5},{8,10},{9,11},{10,... | collective-permute-start | bytes 110600 | tf_op jit(solution)/shard_map/ppermute | solution.py:63
  78.5 4.2 %fusion.25 = bf16[1,128,16,512]{1,3,2,0:T(8,128)(2,1)} fusion(bf16[1,16,128,512]{2,3,1,0:T(8,128)(2,1)} %copy-done.3, bf16[512,576]{1,0:T(8,128)(2,1)S(1)} %constant_dynamic-update-slice_fusion), kind=kOutput, calls=%fused_computation.29 | convolution fusion | flops 1075838976 | bytes 4718592 | tf_op jit(solution)/shard_map/shtj,sjd->sthd/dot_general | solution.py:106
  82.7 0.0 collective-permute-done.10
  82.7 1.6 %collective-permute-start.11 = (bf16[2,2,16,576]{3,2,0,1:T(8,128)(2,1)S(1)}, bf16[2,2,16,576]{3,2,0,1:T(8,128)(2,1)S(1)}, u32[]{:S(2)}, u32[]{:S(2)}) collective-permute-start(bf16[2,2,16,576]{3,2,0,1:T(8,128)(2,1)S(1)} %pad_maximum_fusion.2), channel_id=1, source_target_pairs={{0,1},{1,0},{2,3},{3,2},{4,5},{5,4},{6,7},{7,6},{8,9},{9,8},{10,11... | collective-permute-start | bytes 221192 | tf_op jit(solution)/shard_map/ppermute | solution.py:63
  84.3 0.0 copy-done.4
  84.3 1.2 %fusion.60 = bf16[1,16,64,128]{3,2,1,0:T(8,128)(2,1)} fusion(bf16[1,16,128,512]{2,3,1,0:T(8,128)(2,1)S(1)} %copy-done.4, bf16[512,576]{1,0:T(8,128)(2,1)S(1)} %constant_dynamic-update-slice_fusion), kind=kOutput, calls=%fused_computation.42 | convolution fusion | flops 134479872 | bytes 2490368 | tf_op jit(solution)/shard_map/shtj,sdj->shdt/dot_general | solution.py:110
  85.6 4.5 %copy.70 = bf16[1,128,16,512]{3,2,1,0:T(8,128)(2,1)} copy(bf16[1,128,16,512]{1,3,2,0:T(8,128)(2,1)} %bitcast.193) | data formatting | bytes 4194304
  90.0 4.5 %copy.71 = bf16[1,128,16,512]{3,2,1,0:T(8,128)(2,1)} copy(bf16[1,128,16,512]{1,3,2,0:T(8,128)(2,1)} %fusion.25) | data formatting | bytes 4194304
  94.5 0.0 collective-permute-done.11
  94.6 0.7 slice_bitcast_fusion.5
  95.3 0.7 copy.72
  (18 shorter events, 0.3 us)
Async XLA Ops:
  0.6 12.2 %copy-start = (bf16[1,128,16,512]{3,2,1,0:T(8,128)(2,1)S(1)}, bf16[1,128,16,512]{3,2,1,0:T(8,128)(2,1)}, u32[]{:S(2)}) copy-start(bf16[1,128,16,512]{3,2,1,0:T(8,128)(2,1)} %param.13) | copy-start | bytes 6291460
  2.6 5.4 %collective-permute-start = (bf16[128,576]{1,0:T(8,128)(2,1)S(1)}, bf16[128,576]{1,0:T(8,128)(2,1)S(1)}, u32[]{:S(2)}, u32[]{:S(2)}) collective-permute-start(bf16[128,576]{1,0:T(8,128)(2,1)S(1)} %get-tuple-element.73), channel_id=1, source_target_pairs={{0,8},{8,16},{16,24},{24,0},{1,9},{9,17},{17,25},{25,1},{2,10},{10... | collective-permute-start | bytes 442376 | tf_op jit(solution)/shard_map/ppermute | solution.py:19
  3.1 6.6 %collective-permute-start.1 = (bf16[128,576]{1,0:T(8,128)(2,1)S(1)}, bf16[128,576]{1,0:T(8,128)(2,1)S(1)}, u32[]{:S(2)}, u32[]{:S(2)}) collective-permute-start(bf16[128,576]{1,0:T(8,128)(2,1)S(1)} %get-tuple-element.73), channel_id=1, source_target_pairs={{0,24},{8,0},{16,8},{24,16},{1,25},{9,1},{17,9},{25,17},{2,26},{10... | collective-permute-start | bytes 442376 | tf_op jit(solution)/shard_map/ppermute | solution.py:24
  8.1 4.7 %collective-permute-start.2 = (bf16[128,576]{1,0:T(8,128)(2,1)S(1)}, bf16[128,576]{1,0:T(8,128)(2,1)S(1)}, u32[]{:S(2)}, u32[]{:S(2)}) collective-permute-start(bf16[128,576]{1,0:T(8,128)(2,1)S(1)} %collective-permute-done), channel_id=1, source_target_pairs={{0,8},{8,16},{16,24},{24,0},{1,9},{9,17},{17,25},{25,1},{2,10},{10... | collective-permute-start | bytes 442376 | tf_op jit(solution)/shard_map/ppermute | solution.py:19
  12.9 2.8 %copy-start.6 = (bf16[1,16,64,128]{3,2,1,0:T(8,128)(2,1)S(1)}, bf16[1,16,64,128]{3,2,1,0:T(8,128)(2,1)}, u32[]{:S(2)}) copy-start(bf16[1,16,64,128]{3,2,1,0:T(8,128)(2,1)} %param.14) | copy-start | bytes 786436
  16.6 4.7 %copy-start.1 = (f32[1,16,128,512]{2,3,1,0:T(8,128)}, f32[1,16,128,512]{2,3,1,0:T(8,128)S(1)}, u32[]{:S(2)}) copy-start(f32[1,16,128,512]{2,3,1,0:T(8,128)S(1)} %get-tuple-element.80) | copy-start | bytes 12582916
  30.2 5.8 %copy-start.2 = (f32[1,16,128,512]{2,3,1,0:T(8,128)S(1)}, f32[1,16,128,512]{2,3,1,0:T(8,128)}, u32[]{:S(2)}) copy-start(f32[1,16,128,512]{2,3,1,0:T(8,128)} %copy-done.1) | copy-start | bytes 12582916
  30.2 5.8 %copy-start.5 = (bf16[1,128,16,512]{3,2,1,0:T(8,128)(2,1)S(1)}, bf16[1,128,16,512]{3,2,1,0:T(8,128)(2,1)}, u32[]{:S(2)}) copy-start(bf16[1,128,16,512]{3,2,1,0:T(8,128)(2,1)} %param.17) | copy-start | bytes 6291460
  39.4 1.3 %copy-start.3 = (bf16[1,16,128,512]{2,3,1,0:T(8,128)(2,1)}, bf16[1,16,128,512]{2,3,1,0:T(8,128)(2,1)S(1)}, u32[]{:S(2)}) copy-start(bf16[1,16,128,512]{2,3,1,0:T(8,128)(2,1)S(1)} %fusion.1) | copy-start | bytes 6291460
  44.3 6.9 %collective-permute-start.5 = (bf16[128,576]{1,0:T(8,128)(2,1)}, bf16[128,576]{1,0:T(8,128)(2,1)}, u32[]{:S(2)}, u32[]{:S(2)}) collective-permute-start(bf16[128,576]{1,0:T(8,128)(2,1)} %get-tuple-element.70), channel_id=1, source_target_pairs={{24,0},{25,1},{26,2},{27,3},{28,4},{29,5},{30,6},{31,7}} | collective-permute-start | bytes 442376 | tf_op jit(solution)/shard_map/ppermute | solution.py:39
  45.6 9.9 %collective-permute-start.4 = (bf16[128,576]{1,0:T(8,128)(2,1)}, bf16[128,576]{1,0:T(8,128)(2,1)}, u32[]{:S(2)}, u32[]{:S(2)}) collective-permute-start(bf16[128,576]{1,0:T(8,128)(2,1)} %get-tuple-element.69), channel_id=1, source_target_pairs={{16,0},{24,8},{17,1},{25,9},{18,2},{26,10},{19,3},{27,11},{20,4},{... | collective-permute-start | bytes 442376 | tf_op jit(solution)/shard_map/ppermute | solution.py:39
  46.9 8.7 %collective-permute-start.3 = (bf16[128,576]{1,0:T(8,128)(2,1)}, bf16[128,576]{1,0:T(8,128)(2,1)}, u32[]{:S(2)}, u32[]{:S(2)}) collective-permute-start(bf16[128,576]{1,0:T(8,128)(2,1)} %get-tuple-element.68), channel_id=1, source_target_pairs={{8,0},{16,8},{24,16},{9,1},{17,9},{25,17},{10,2},{18,10},{26,18},{... | collective-permute-start | bytes 442376 | tf_op jit(solution)/shard_map/ppermute | solution.py:39
  56.7 0.7 copy-start.7
  57.4 4.8 %collective-permute-start.6 = (bf16[2,2,16,576]{3,2,1,0:T(8,128)(2,1)S(1)}, bf16[2,2,16,576]{3,2,1,0:T(8,128)(2,1)S(1)}, u32[]{:S(2)}, u32[]{:S(2)}) collective-permute-start(bf16[2,2,16,576]{3,2,1,0:T(8,128)(2,1)S(1)} %bitcast_convert_fusion.1), channel_id=1, source_target_pairs={{0,1},{1,0},{2,3},{3,2},{4,5},{5,4},{6,7},{7,6},{8,9},{9,8},{10,11... | collective-permute-start | bytes 221192 | tf_op jit(solution)/shard_map/ppermute | solution.py:56
  63.2 4.1 %collective-permute-start.7 = (bf16[2,16,576]{2,1,0:T(8,128)(2,1)S(1)}, bf16[2,16,576]{2,1,0:T(8,128)(2,1)S(1)}, u32[]{:S(2)}, u32[]{:S(2)}) collective-permute-start(bf16[2,16,576]{2,1,0:T(8,128)(2,1)S(1)} %bitcast_convert_fusion.2), channel_id=1, source_target_pairs={{0,2},{1,3},{2,0},{3,1},{4,6},{5,7},{6,4},{7,5},{8,10},{9,11},{10,... | collective-permute-start | bytes 110600 | tf_op jit(solution)/shard_map/ppermute | solution.py:56
  67.3 4.7 %collective-permute-start.8 = (bf16[16,576]{1,0:T(8,128)(2,1)S(1)}, bf16[16,576]{1,0:T(8,128)(2,1)S(1)}, u32[]{:S(2)}, u32[]{:S(2)}) collective-permute-start(bf16[16,576]{1,0:T(8,128)(2,1)S(1)} %bitcast_convert_fusion.3), channel_id=1, source_target_pairs={{0,4},{1,5},{2,6},{3,7},{4,0},{5,1},{6,2},{7,3},{8,12},{9,13},{10,... | collective-permute-start | bytes 55304 | tf_op jit(solution)/shard_map/ppermute | solution.py:56
  72.1 4.9 %collective-permute-start.9 = (bf16[16,576]{1,0:T(8,128)(2,1)S(1)}, bf16[16,576]{1,0:T(8,128)(2,1)S(1)}, u32[]{:S(2)}, u32[]{:S(2)}) collective-permute-start(bf16[16,576]{1,0:T(8,128)(2,1)S(1)} %fusion.90), channel_id=1, source_target_pairs={{0,4},{1,5},{2,6},{3,7},{4,0},{5,1},{6,2},{7,3},{8,12},{9,13},{10,... | collective-permute-start | bytes 55304 | tf_op jit(solution)/shard_map/ppermute | solution.py:63
  74.7 9.6 %copy-start.4 = (bf16[1,16,128,512]{2,3,1,0:T(8,128)(2,1)S(1)}, bf16[1,16,128,512]{2,3,1,0:T(8,128)(2,1)}, u32[]{:S(2)}) copy-start(bf16[1,16,128,512]{2,3,1,0:T(8,128)(2,1)} %copy-done.3) | copy-start | bytes 6291460
  77.0 5.7 %collective-permute-start.10 = (bf16[2,16,576]{2,1,0:T(8,128)(2,1)S(1)}, bf16[2,16,576]{2,1,0:T(8,128)(2,1)S(1)}, u32[]{:S(2)}, u32[]{:S(2)}) collective-permute-start(bf16[2,16,576]{2,1,0:T(8,128)(2,1)S(1)} %pad_maximum_fusion.3), channel_id=1, source_target_pairs={{0,2},{1,3},{2,0},{3,1},{4,6},{5,7},{6,4},{7,5},{8,10},{9,11},{10,... | collective-permute-start | bytes 110600 | tf_op jit(solution)/shard_map/ppermute | solution.py:63
  82.7 11.8 %collective-permute-start.11 = (bf16[2,2,16,576]{3,2,0,1:T(8,128)(2,1)S(1)}, bf16[2,2,16,576]{3,2,0,1:T(8,128)(2,1)S(1)}, u32[]{:S(2)}, u32[]{:S(2)}) collective-permute-start(bf16[2,2,16,576]{3,2,0,1:T(8,128)(2,1)S(1)} %pad_maximum_fusion.2), channel_id=1, source_target_pairs={{0,1},{1,0},{2,3},{3,2},{4,5},{5,4},{6,7},{7,6},{8,9},{9,8},{10,11... | collective-permute-start | bytes 221192 | tf_op jit(solution)/shard_map/ppermute | solution.py:63
